TPU v7x, 128 devices: a whole 4x4x4 slice. The times are simulated.
128 devices in a mesh: band: 4 (over x), pair: 32 (over z, y, core).
Axes of the slice: x: 4, y: 4, z: 4, core: 2. Of those that a mesh axis runs over, the one named last changes fastest.
Arguments:
- traces: float32 [16, 8192, 1024], P('band', 'pair'), may hold values from -300 to 300
- pair_list: int32 [256, 2], replicated, may hold values from 0 to 63, as said below
- pair_owner: int32 [256], replicated, may hold values from 0 to 63, as said below
Outputs:
- cross_spectra: bfloat16 [64, 2, 128, 128, 512], P('pair', None, None, None, 'band')
Inputs may be any that keep to these rules, and one draw needn't show every extreme that they name: `pair_list`: each row (i, j) has 8 <= j - i <= 24; index p of pair holds blocks p * 64 / 32 up to (p + 1) * 64 / 32 - 1, and the 16 blocks named by the rows of one owner (pair_owner // 2) all lie on different indices of pair. `pair_owner`: every slot is named by exactly 4 rows.
All inputs are finite; a program needn't handle non-finite values.
Results may differ from a plain program's by a relative error of at most 0.0057.
Values may be sent and summed in bfloat16 or wider, within the bound.
No kernel may reach another device: no remote copies, remote signals or barrier semaphores. Data moves between devices by JAX's collectives and lax.ppermute only.
A program may use at most 320 MiB of HBM per device.

v0:
```python
import jax
import jax.numpy as jnp
from jax import lax
from jax.sharding import PartitionSpec as P

SUB = 64
BLOCK = 128
SLOTS = 2


whiten_eps = 1e-05


def dft_table(samples, bin_count):
    sample_ids = lax.broadcasted_iota(jnp.int32, (samples, bin_count), 0)
    bin_ids = lax.broadcasted_iota(jnp.int32, (samples, bin_count), 1)
    phase_angle = (sample_ids * bin_ids % samples).astype(jnp.float32) * (2.0 * jnp.pi / samples)
    return jnp.concatenate([jnp.cos(phase_angle), -jnp.sin(phase_angle)], axis=1)


def whiten(flat_traces, bin_count):
    row_count, samples = flat_traces.shape
    spectra = jnp.dot(
        flat_traces,
        dft_table(samples, bin_count),
        precision=lax.Precision.HIGHEST,
        preferred_element_type=jnp.float32,
    )
    real_band = spectra[:, :bin_count].reshape(row_count, bin_count // SUB, SUB)
    imag_band = spectra[:, bin_count:].reshape(row_count, bin_count // SUB, SUB)
    band_power = jnp.mean(real_band * real_band + imag_band * imag_band, axis=-1, keepdims=True)
    factor = lax.rsqrt(band_power + whiten_eps)
    stacked = jnp.stack([real_band * factor, imag_band * factor], axis=1)
    return stacked.reshape(row_count, 2, bin_count).astype(jnp.bfloat16)


def shards(traces, pair_list, pair_owner):
    win_local, chan_local, samples = traces.shape
    bin_count = samples // 2
    owners = lax.axis_size("pair")
    per_device = chan_local // BLOCK
    per_slot = pair_list.shape[0] // (owners * SLOTS)
    whitened = whiten(traces.reshape(win_local * chan_local, samples), bin_count)
    whitened = whitened.reshape(win_local, per_device, BLOCK, 2, bin_count)
    device_index = lax.axis_index("pair")
    first_blocks = pair_list[:, 0]
    second_blocks = pair_list[:, 1]
    owner_of = pair_owner // SLOTS
    local_ids = device_index * per_device + jnp.arange(per_device, dtype=jnp.int32)
    owner_ids = jnp.arange(owners, dtype=jnp.int32)
    holds_block = (
        (first_blocks[:, None] == local_ids[None, :])
        | (second_blocks[:, None] == local_ids[None, :])
    ).astype(jnp.int32)
    belongs = (owner_of[:, None] == owner_ids[None, :]).astype(jnp.int32)
    wanted = jnp.minimum(jnp.dot(belongs.T, holds_block), 1)
    send_index = jnp.sum(wanted * jnp.arange(per_device, dtype=jnp.int32)[None, :], axis=1)
    send_mask = jnp.minimum(jnp.sum(wanted, axis=1), 1).astype(jnp.bfloat16)
    slot_ids = device_index * SLOTS + jnp.arange(SLOTS, dtype=jnp.int32)
    slot_match = (pair_owner[:, None] == slot_ids[None, :]).astype(jnp.int32)
    slot_rank = jnp.cumsum(slot_match, axis=0) - 1
    rank_ids = jnp.arange(per_slot, dtype=jnp.int32)
    selected = slot_match[:, :, None] * (slot_rank[:, :, None] == rank_ids[None, None, :]).astype(
        jnp.int32
    )
    source_first = jnp.sum(selected * first_blocks[:, None, None], axis=0) // per_device
    source_second = jnp.sum(selected * second_blocks[:, None, None], axis=0) // per_device
    relaid = lax.all_to_all(whitened, "band", split_axis=4, concat_axis=0, tiled=True)
    outgoing = jnp.take(relaid, send_index, axis=1) * send_mask[None, :, None, None, None]
    received = lax.all_to_all(outgoing, "pair", split_axis=1, concat_axis=1, tiled=True)
    results = []
    for slot_number in range(SLOTS):
        left_rows = jnp.take(received, source_first[slot_number], axis=1)
        right_rows = jnp.take(received, source_second[slot_number], axis=1)
        rotated = jnp.stack([left_rows[:, :, :, 1], -left_rows[:, :, :, 0]], axis=3)
        paired = jnp.stack([left_rows, rotated], axis=2)
        product = jnp.einsum(
            "wtcakf,wtbkf->cabf", paired, right_rows, preferred_element_type=jnp.float32
        )
        results.append(product)
    return jnp.stack(results).astype(jnp.bfloat16)


def solution(mesh):
    placed = (P("band", "pair", None), P(), P())
    return jax.shard_map(
        shards,
        mesh=mesh,
        in_specs=placed,
        out_specs=P("pair", None, None, None, "band"),
        check_vma=False,
    )
```

profile of v0, /device:TPU:0, one launch (start us, length us, event | category | flops | bytes accessed | tf_op | source)
XLA Modules:
  0.0 735.3 jit_solution(655517419393215909)
XLA Ops:
  0.0 8.2 %sine_negate_fusion = (f32[1024,512]{1,0:T(8,128)S(1)}, f32[1024,512]{1,0:T(8,128)S(1)}) fusion(), kind=kLoop, calls=%fused_computation.41 | loop fusion | flops 7864320 | bytes 4194304 | tf_op jit(solution)/shard_map/neg | solution.py:18
  8.3 14.8 %fusion.16 = f32[1024,1024]{1,0:T(8,128)S(1)} fusion(f32[1024,1024]{1,0:T(8,128)S(1)} %bitcast.103, f32[1024,512]{1,0:T(8,128)S(1)} %get-tuple-element.34, f32[1024,512]{1,0:T(8,128)S(1)} %get-tuple-element.35), kind=kOutput, calls=%fused_computation.30 | convolution fusion | flops 12885950464 | bytes 12582912 | tf_op jit(solution)/shard_map/dot_general | solution.py:23
  36.7 4.7 copy.59
  45.2 6.7 pad_maximum_fusion.1
  56.7 26.0 %all-to-all-done = bf16[4,2,128,2,512]{2,3,1,0,4:T(2,128)(2,1)S(1)} async-done(((bf16[4,2,128,2,512]{2,3,1,0,4:T(2,128)(2,1)}), bf16[4,2,128,2,512]{2,3,1,0,4:T(2,128)(2,1)S(1)}, u32[]{:S(2)}, u32[]{:S(2)}) %all-to-all-start) | async-done | bytes 2097184 | tf_op jit(solution)/shard_map/all_to_all | solution.py:68
  87.6 12.1 %gather_fusion = bf16[32,16,128,2,128]{4,2,3,1,0:T(8,128)(2,1)} fusion(bf16[16,2,128,2,128]{4,2,3,1,0:T(8,128)(2,1)S(1)} %bitcast.91, s32[1024]{0:T(1024)S(1)} %pad_clamp_fusion.4), kind=kCustom, calls=%fused_computation.4 | custom fusion | bytes 67108992 | tf_op jit(solution)/shard_map/jit(_take)/gather | solution.py:69
  99.6 22.9 %multiply_bitcast_fusion = bf16[16,32,128,2,128]{4,2,3,0,1:T(8,128)(2,1)} fusion(bf16[32,16,128,2,128]{4,2,3,1,0:T(8,128)(2,1)} %gather_fusion, pred[32]{0:T(512)(128)(4,1)S(1)} %compare_and_fusion.4, bf16[32]{0:T(256)(128)(2,1)S(1)} %minimum_convert_fusion), kind=kLoop, calls=%fused_computation.5 | loop fusion | flops 33554432 | bytes 67108960 | tf_op jit(solution)/shard_map/mul | solution.py:69
  122.5 8.9 %all-to-all-start.1 = ((bf16[16,32,128,2,128]{4,2,3,0,1:T(8,128)(2,1)}), bf16[16,32,128,2,128]{4,2,3,0,1:T(8,128)(2,1)}, u32[]{:S(2)}, u32[]{:S(2)}) async-start(bf16[16,32,128,2,128]{4,2,3,0,1:T(8,128)(2,1)} %multiply_bitcast_fusion), calls=%async_computation.1 | async-start | bytes 67108864 | tf_op jit(solution)/shard_map/all_to_all | solution.py:70
  132.9 437.7 %all-to-all-done.1 = bf16[16,32,128,2,128]{4,2,3,0,1:T(8,128)(2,1)} async-done(((bf16[16,32,128,2,128]{4,2,3,0,1:T(8,128)(2,1)}), bf16[16,32,128,2,128]{4,2,3,0,1:T(8,128)(2,1)}, u32[]{:S(2)}, u32[]{:S(2)}) %all-to-all-start.1) | async-done | bytes 33554464 | tf_op jit(solution)/shard_map/all_to_all | solution.py:70
  570.6 22.9 %copy.63 = bf16[16,32,128,2,128]{4,2,3,1,0:T(8,128)(2,1)} copy(bf16[16,32,128,2,128]{4,2,3,0,1:T(8,128)(2,1)} %all-to-all-done.1) | data formatting | bytes 67108864 | tf_op jit(solution)/shard_map/all_to_all | solution.py:70
  593.5 5.0 gather_fusion.2
  598.5 7.9 %copy.65 = bf16[4,16,128,2,128]{2,1,0,3,4:T(8,128)(2,1)} copy(bf16[4,16,128,2,128]{4,2,3,1,0:T(8,128)(2,1)} %gather_fusion.2) | data formatting | bytes 8388608 | tf_op jit(solution)/shard_map/jit(_take)/gather | solution.py:73
  606.4 4.7 fusion.25
  612.9 5.0 gather_fusion.1
  622.6 7.9 %copy.74 = bf16[16,4,128,2,128,1]{2,0,1,3,5,4:T(8,128)(2,1)} copy(bf16[16,4,128,2,128,1]{4,2,3,0,1,5:T(8,128)(2,1)} %select_bitcast_fusion.1) | data formatting | bytes 8388608 | tf_op jit(solution)/shard_map/jit(_take)/select_n | solution.py:74
  630.5 5.0 gather_fusion.4
  635.5 7.9 %copy.70 = bf16[4,16,128,2,128]{2,1,0,3,4:T(8,128)(2,1)} copy(bf16[4,16,128,2,128]{4,2,3,1,0:T(8,128)(2,1)} %gather_fusion.4) | data formatting | bytes 8388608 | tf_op jit(solution)/shard_map/jit(_take)/gather | solution.py:73
  643.5 4.7 fusion.27
  650.5 5.0 gather_fusion.3
  660.2 8.1 %copy.76 = bf16[16,4,128,2,128,1]{2,0,1,3,5,4:T(8,128)(2,1)} copy(bf16[16,4,128,2,128,1]{4,2,3,0,1,5:T(8,128)(2,1)} %select_bitcast_fusion) | data formatting | bytes 8388608 | tf_op jit(solution)/shard_map/jit(_take)/select_n | solution.py:74
  674.8 10.3 %fusion.6 = bf16[1,2,128,128,128]{2,3,1,4,0:T(8,128)(2,1)} fusion(bf16[16,4,128,2,128,1]{2,0,1,3,5,4:T(8,128)(2,1)} %copy.74, bf16[16,4,1,128,2,128]{3,0,1,4,2,5:T(8,128)(2,1)} %maximum_bitcast_fusion, bf16[16,4,1,128,2,128]{3,0,1,4,2,5:T(8,128)(2,1)} %get-tuple-element.20), kind=kOutput, calls=%fused_computation.15 | convolution fusion | flops 1094713344 | bytes 20971520 | tf_op jit(solution)/shard_map/wtcakf,wtbkf->cabf/dot_general | solution.py:77
  685.1 10.4 %fusion.9 = bf16[1,2,128,128,128]{2,3,1,4,0:T(8,128)(2,1)} fusion(bf16[16,4,128,2,128,1]{2,0,1,3,5,4:T(8,128)(2,1)} %copy.76, bf16[16,4,1,128,2,128]{3,0,1,4,2,5:T(8,128)(2,1)} %maximum_bitcast_fusion.1, bf16[16,4,1,128,2,128]{3,0,1,4,2,5:T(8,128)(2,1)} %get-tuple-element.22), kind=kOutput, calls=%fused_computation.16 | convolution fusion | flops 1094713344 | bytes 20971520 | tf_op jit(solution)/shard_map/wtcakf,wtbkf->cabf/dot_general | solution.py:77
  695.5 13.7 %pad_maximum_fusion = bf16[2,2,128,128,128]{2,3,1,4,0:T(8,128)(2,1)} fusion(bf16[1,2,128,128,128]{2,3,1,4,0:T(8,128)(2,1)} %fusion.9, bf16[1,2,128,128,128]{2,3,1,4,0:T(8,128)(2,1)} %fusion.6), kind=kLoop, calls=%fused_computation.6 | loop fusion | flops 8388608 | bytes 33554432 | tf_op jit(solution)/shard_map/stack | solution.py:81
  709.3 25.8 %copy.73 = bf16[2,2,128,128,128]{4,3,2,1,0:T(8,128)(2,1)} copy(bf16[2,2,128,128,128]{2,3,1,4,0:T(8,128)(2,1)} %pad_maximum_fusion) | data formatting | bytes 33554432 | tf_op jit(solution)/shard_map/stack | solution.py:81
  (52 shorter events, 48.2 us)
Async XLA Ops:
  0.0 8.2 %copy-start.5 = (f32[4,256,1024]{2,1,0:T(8,128)S(1)}, f32[4,256,1024]{2,1,0:T(8,128)}, u32[]{:S(2)}) copy-start(f32[4,256,1024]{2,1,0:T(8,128)} %param.5) | copy-start | bytes 12582916
  23.1 2.0 copy-start
  45.2 11.1 %copy-start.3 = (s32[256]{0:T(256)S(1)}, s32[256]{0:T(256)}, u32[]{:S(2)}) copy-start(s32[256]{0:T(256)} %param.7) | copy-start | bytes 3076
  45.2 11.2 %copy-start.4 = (s32[256,2]{0,1:T(2,128)S(1)}, s32[256,2]{0,1:T(2,128)}, u32[]{:S(2)}) copy-start(s32[256,2]{0,1:T(2,128)} %param.6) | copy-start | bytes 6148
  52.0 30.7 %all-to-all-start = ((bf16[4,2,128,2,512]{2,3,1,0,4:T(2,128)(2,1)}), bf16[4,2,128,2,512]{2,3,1,0,4:T(2,128)(2,1)S(1)}, u32[]{:S(2)}, u32[]{:S(2)}) async-start(bf16[4,2,128,2,512]{2,3,1,0,4:T(2,128)(2,1)} %pad_maximum_fusion.1), calls=%async_computation | async-start | bytes 4194304 | tf_op jit(solution)/shard_map/all_to_all | solution.py:68
  122.5 448.1 %all-to-all-start.1 = ((bf16[16,32,128,2,128]{4,2,3,0,1:T(8,128)(2,1)}), bf16[16,32,128,2,128]{4,2,3,0,1:T(8,128)(2,1)}, u32[]{:S(2)}, u32[]{:S(2)}) async-start(bf16[16,32,128,2,128]{4,2,3,0,1:T(8,128)(2,1)} %multiply_bitcast_fusion), calls=%async_computation.1 | async-start | bytes 67108864 | tf_op jit(solution)/shard_map/all_to_all | solution.py:70
  668.3 4.2 copy-start.1
  668.4 4.2 copy-start.2
where the time goes:
time: 746 us; the launch traced here: 735 us
  waiting for transfers between devices  464 us (62%)
  local copies, waits for them, and re-layouts  133 us (18%)
  other arithmetic  89.1 us (12%)
  matrix products  35.8 us (5%)
  starting transfers between devices  13.3 us (2%)
    all_to_all x1, waiting for transfers between devices, shards(): lax.all_to_all(outgoing, 'pair', split_axis=1, concat_axis=1, tiled=True)  438 us
    all_to_all x1, waiting for transfers between devices, shards(): lax.all_to_all(whitened, 'band', split_axis=4, concat_axis=0, tiled=True)  26 us
    gather x4, local copies, waits for them, and re-layouts, shards(): left_rows = jnp.take(received, source_first[slot_number], axis=1)  25.9 us
    another operation x1, local copies, waits for them, and re-layouts, shards(): return jnp.stack(results).astype(jnp.bfloat16)  25.8 us
    all_to_all x1, local copies, waits for them, and re-layouts, shards(): lax.all_to_all(outgoing, 'pair', split_axis=1, concat_axis=1, tiled=True)  22.9 us
    mul x1, other arithmetic, shards(): jnp.take(relaid, send_index, axis=1) * send_mask[None, :, None, None, None]  22.9 us
    dot_general x2, matrix products, shards(): jnp.einsum('wtcakf,wtbkf->cabf', paired, right_rows, preferred_element_ty...  20.7 us
    select_n x2, local copies, waits for them, and re-layouts, shards(): right_rows = jnp.take(received, source_second[slot_number], axis=1)  16.1 us
  transfers between devices with their start and end apart: 2, of which 2 were waited for; matrix products, arithmetic and copies ran while one was open for 0% of the time, Pallas kernels for 0%

commit v1 on v0

v1 whole, which is shorter than its diff:
```python
import jax
import jax.numpy as jnp
from jax import lax
from jax.sharding import PartitionSpec as P

SUB = 64
BLOCK = 128
SLOTS = 2
CHUNKS = 4


whiten_eps = 1e-05


def dft_table(samples, bin_count):
    sample_ids = lax.broadcasted_iota(jnp.int32, (samples, bin_count), 0)
    bin_ids = lax.broadcasted_iota(jnp.int32, (samples, bin_count), 1)
    phase_angle = (sample_ids * bin_ids % samples).astype(jnp.float32) * (2.0 * jnp.pi / samples)
    return jnp.concatenate([jnp.cos(phase_angle), -jnp.sin(phase_angle)], axis=1)


def whiten(flat_traces, bin_count):
    row_count, samples = flat_traces.shape
    spectra = jnp.dot(
        flat_traces,
        dft_table(samples, bin_count),
        precision=lax.Precision.HIGHEST,
        preferred_element_type=jnp.float32,
    )
    real_band = spectra[:, :bin_count].reshape(row_count, bin_count // SUB, SUB)
    imag_band = spectra[:, bin_count:].reshape(row_count, bin_count // SUB, SUB)
    band_power = jnp.mean(real_band * real_band + imag_band * imag_band, axis=-1, keepdims=True)
    factor = lax.rsqrt(band_power + whiten_eps)
    stacked = jnp.stack([real_band * factor, imag_band * factor], axis=1)
    return stacked.reshape(row_count, 2, bin_count).astype(jnp.bfloat16)


def slot_blocks(pair_list, pair_owner, slot_ids, per_slot):
    slot_match = (pair_owner[:, None] == slot_ids[None, :]).astype(jnp.int32)
    slot_rank = jnp.cumsum(slot_match, axis=0) - 1
    rank_ids = jnp.arange(per_slot, dtype=jnp.int32)
    selected = slot_match[:, :, None] * (slot_rank[:, :, None] == rank_ids[None, None, :]).astype(jnp.int32)
    first = jnp.sum(selected * pair_list[:, 0][:, None, None], axis=0)
    second = jnp.sum(selected * pair_list[:, 1][:, None, None], axis=0)
    return first, second


def shards(traces, pair_list, pair_owner):
    win_local, chan_local, samples = traces.shape
    bin_count = samples // 2
    bands = lax.axis_size("band")
    owners = lax.axis_size("pair")
    band_bins = bin_count // bands
    per_device = chan_local // BLOCK
    per_slot = pair_list.shape[0] // (owners * SLOTS)
    chunk = band_bins // CHUNKS

    whitened = whiten(traces.reshape(win_local * chan_local, samples), bin_count)
    whitened = whitened.reshape(win_local, per_device, BLOCK, 2, bands, band_bins)
    whitened = jnp.transpose(whitened, (4, 1, 3, 0, 5, 2))
    relaid = lax.all_to_all(whitened, "band", split_axis=0, concat_axis=0, tiled=True)

    device_index = lax.axis_index("pair")
    slot_ids = device_index * SLOTS + jnp.arange(SLOTS, dtype=jnp.int32)
    first, second = slot_blocks(pair_list, pair_owner, slot_ids, per_slot)

    out = jnp.zeros((SLOTS, 2, BLOCK, BLOCK, band_bins), jnp.bfloat16)
    for part in range(CHUNKS):
        piece = relaid[:, :, :, :, part * chunk:(part + 1) * chunk, :]
        gathered = lax.all_gather(piece, "pair", axis=1, tiled=True)
        left = jnp.take(gathered, first.reshape(-1), axis=1)
        left = left.reshape(left.shape[0], SLOTS, per_slot, *left.shape[2:])
        left = jnp.moveaxis(left, 1, 0)
        right = jnp.take(gathered, second.reshape(-1), axis=1)
        right = right.reshape(right.shape[0], SLOTS, per_slot, *right.shape[2:])
        right = jnp.moveaxis(right, 1, 0)
        rotated = jnp.stack([-right[:, :, :, 1], right[:, :, :, 0]], axis=3)
        paired = jnp.stack([right, rotated], axis=1)
        product = jnp.einsum(
            "sgtkwfa,spgtkwfb->spabf", left, paired, preferred_element_type=jnp.float32
        )
        out = lax.dynamic_update_slice_in_dim(out, product.astype(jnp.bfloat16), part * chunk, axis=4)
    return out


def solution(mesh):
    placed = (P("band", "pair", None), P(), P())
    return jax.shard_map(
        shards,
        mesh=mesh,
        in_specs=placed,
        out_specs=P("pair", None, None, None, "band"),
        check_vma=False,
    )
```

time: 746 us -> 534 us (0.72)
  the two profiles are of different devices: /device:TPU:0 before, /device:TPU:1 now
where the time goes in v1:
time: 534 us; the launch traced here: 526 us
  waiting for transfers between devices  274 us (51%)
  local copies, waits for them, and re-layouts  102 us (19%)
  matrix products  71.1 us (13%)
  other arithmetic  35.2 us (7%)
  blocking collectives  30.1 us (6%)
  between operations  13.9 us (3%)
    all_gather x4, waiting for transfers between devices, shards(): gathered = lax.all_gather(piece, 'pair', axis=1, tiled=True)  272 us
    dot_general x1, matrix products, whiten(): jnp.dot(flat_traces, dft_table(samples, bin_count), precision=lax.Precisi...  38.6 us
    dot_general x4, matrix products, shards(): jnp.einsum('sgtkwfa,spgtkwfb->spabf', left, paired, preferred_element_typ...  32.5 us
    dynamic_update_slice x2, local copies, waits for them, and re-layouts, shards(): lax.dynamic_update_slice_in_dim(out, product.astype(jnp.bfloat16), part *...  32.5 us
    gather x4, local copies, waits for them, and re-layouts, shards(): right = jnp.take(gathered, second.reshape(-1), axis=1)  30.5 us
    gather x4, local copies, waits for them, and re-layouts, shards(): left = jnp.take(gathered, first.reshape(-1), axis=1)  30.5 us
    all_to_all x1, blocking collectives, shards(): lax.all_to_all(whitened, 'band', split_axis=0, concat_axis=0, tiled=True)  30.1 us
    another operation x4, other arithmetic, shards(): paired = jnp.stack([right, rotated], axis=1)  11 us
  transfers between devices with their start and end apart: 4, of which 4 were waited for; matrix products, arithmetic and copies ran while one was open for 5% of the time, Pallas kernels for 0%

profile of v1, /device:TPU:1, one launch (start us, length us, event | category | flops | bytes accessed | tf_op | source)
XLA Modules:
  0.0 526.4 jit_solution(5466479605399662637)
XLA Ops:
  6.5 8.2 %sine_negate_fusion = (f32[1024,512]{1,0:T(8,128)S(1)}, f32[1024,512]{1,0:T(8,128)S(1)}) fusion(), kind=kLoop, calls=%fused_computation.61 | loop fusion | flops 7864320 | bytes 4194304 | tf_op jit(solution)/shard_map/neg | solution.py:19
  14.8 38.6 %fusion.35 = f32[1024,1024]{0,1:T(8,128)S(1)} fusion(f32[1024,1024]{1,0:T(8,128)S(1)} %bitcast.176, f32[1024,512]{1,0:T(8,128)S(1)} %get-tuple-element.40, f32[1024,512]{1,0:T(8,128)S(1)} %get-tuple-element.41), kind=kOutput, calls=%fused_computation.44 | convolution fusion | flops 12885950464 | bytes 12582912 | tf_op jit(solution)/shard_map/dot_general | solution.py:24
  56.8 30.1 %all_to_all.5 = bf16[4,2,2,4,128,128]{5,4,3,2,1,0:T(8,128)(2,1)S(1)} all-to-all(bf16[4,2,2,4,128,128]{5,4,3,2,1,0:T(8,128)(2,1)S(1)} %maximum_bitcast_fusion), channel_id=1, replica_groups=mesh['band'=4,'pair'=32] {'band'}, dimensions={0} | all-to-all | bytes 4194304 | tf_op jit(solution)/shard_map/all_to_all | solution.py:61
  92.3 71.2 %all-gather.5.cloned.1.call-done = bf16[4,64,2,4,32,128]{5,4,3,2,1,0:T(8,128)(2,1)} async-done(((bf16[4,2,2,4,32,128]{5,4,3,2,1,0:T(8,128)(2,1)}), bf16[4,64,2,4,32,128]{5,4,3,2,1,0:T(8,128)(2,1)}) %all-gather.5.cloned.1.call-update) | async-done | bytes 16777232 | tf_op jit(solution)/shard_map/all_gather | solution.py:70
  163.5 6.7 %gather_fusion = bf16[8,4,2,4,32,128]{5,4,3,2,1,0:T(8,128)(2,1)S(1)} fusion(bf16[4,64,2,4,32,128]{5,4,3,2,1,0:T(8,128)(2,1)} %all-gather.5.cloned.1.call-done, s32[1024]{0:T(1024)S(1)} %pad_clamp_fusion.1), kind=kCustom, calls=%fused_computation.clone | custom fusion | bytes 4194336 | tf_op jit(solution)/shard_map/jit(_take)/gather | solution.py:74
  170.2 67.7 %all-gather.7.cloned.1.call-done = bf16[4,64,2,4,32,128]{5,4,3,2,1,0:T(8,128)(2,1)} async-done(((bf16[4,2,2,4,32,128]{5,4,3,2,1,0:T(8,128)(2,1)}), bf16[4,64,2,4,32,128]{5,4,3,2,1,0:T(8,128)(2,1)}) %all-gather.7.cloned.1.call-update) | async-done | bytes 16777232 | tf_op jit(solution)/shard_map/all_gather | solution.py:70
  237.9 7.9 %gather_fusion.2 = bf16[8,4,2,4,32,128]{5,4,3,2,1,0:T(8,128)(2,1)} fusion(bf16[4,64,2,4,32,128]{5,4,3,2,1,0:T(8,128)(2,1)} %all-gather.7.cloned.1.call-done, s32[1024]{0:T(1024)S(1)} %pad_clamp_fusion.1), kind=kCustom, calls=%fused_computation.2.clone | custom fusion | bytes 4194336 | tf_op jit(solution)/shard_map/jit(_take)/gather | solution.py:74
  245.8 66.5 %all-gather.9.cloned.1.call-done = bf16[4,64,2,4,32,128]{5,4,3,2,1,0:T(8,128)(2,1)} async-done(((bf16[4,2,2,4,32,128]{5,4,3,2,1,0:T(8,128)(2,1)}), bf16[4,64,2,4,32,128]{5,4,3,2,1,0:T(8,128)(2,1)}) %all-gather.9.cloned.1.call-update) | async-done | bytes 16777232 | tf_op jit(solution)/shard_map/all_gather | solution.py:70
  312.3 7.9 %gather_fusion.4 = bf16[8,4,2,4,32,128]{5,4,3,2,1,0:T(8,128)(2,1)} fusion(bf16[4,64,2,4,32,128]{5,4,3,2,1,0:T(8,128)(2,1)} %all-gather.9.cloned.1.call-done, s32[1024]{0:T(1024)S(1)} %pad_clamp_fusion.1), kind=kCustom, calls=%fused_computation.4.clone | custom fusion | bytes 4194336 | tf_op jit(solution)/shard_map/jit(_take)/gather | solution.py:74
  320.2 66.3 %all-gather.11.cloned.1.call-done = bf16[4,64,2,4,32,128]{5,4,3,2,1,0:T(8,128)(2,1)} async-done(((bf16[4,2,2,4,32,128]{5,4,3,2,1,0:T(8,128)(2,1)}), bf16[4,64,2,4,32,128]{5,4,3,2,1,0:T(8,128)(2,1)}) %all-gather.11.cloned.1.call-update) | async-done | bytes 16777232 | tf_op jit(solution)/shard_map/all_gather | solution.py:70
  386.6 7.9 %gather_fusion.6 = bf16[8,4,2,4,32,128]{5,4,3,2,1,0:T(8,128)(2,1)} fusion(bf16[4,64,2,4,32,128]{5,4,3,2,1,0:T(8,128)(2,1)} %all-gather.11.cloned.1.call-done, s32[1024]{0:T(1024)S(1)} %pad_clamp_fusion.1), kind=kCustom, calls=%fused_computation.6.clone | custom fusion | bytes 4194336 | tf_op jit(solution)/shard_map/jit(_take)/gather | solution.py:74
  394.5 3.6 broadcast_select_fusion.4
  409.0 2.9 maximum_bitcast_fusion.3
  417.3 6.7 %gather_fusion.1 = bf16[8,4,2,4,32,128]{5,4,3,2,1,0:T(8,128)(2,1)S(1)} fusion(bf16[4,64,2,4,32,128]{5,4,3,2,1,0:T(8,128)(2,1)} %all-gather.5.cloned.1.call-done, s32[1024]{0:T(1024)S(1)} %pad_clamp_fusion), kind=kCustom, calls=%fused_computation.1.clone | custom fusion | bytes 4194336 | tf_op jit(solution)/shard_map/jit(_take)/gather | solution.py:71
  424.0 7.9 %gather_fusion.3 = bf16[8,4,2,4,32,128]{5,4,3,2,1,0:T(8,128)(2,1)} fusion(bf16[4,64,2,4,32,128]{5,4,3,2,1,0:T(8,128)(2,1)} %all-gather.7.cloned.1.call-done, s32[1024]{0:T(1024)S(1)} %pad_clamp_fusion), kind=kCustom, calls=%fused_computation.3.clone | custom fusion | bytes 4194336 | tf_op jit(solution)/shard_map/jit(_take)/gather | solution.py:71
  431.9 8.0 %gather_fusion.5 = bf16[8,4,2,4,32,128]{5,4,3,2,1,0:T(8,128)(2,1)} fusion(bf16[4,64,2,4,32,128]{5,4,3,2,1,0:T(8,128)(2,1)} %all-gather.9.cloned.1.call-done, s32[1024]{0:T(1024)S(1)} %pad_clamp_fusion), kind=kCustom, calls=%fused_computation.5.clone | custom fusion | bytes 4194336 | tf_op jit(solution)/shard_map/jit(_take)/gather | solution.py:71
  439.9 7.9 %gather_fusion.7 = bf16[8,4,2,4,32,128]{5,4,3,2,1,0:T(8,128)(2,1)} fusion(bf16[4,64,2,4,32,128]{5,4,3,2,1,0:T(8,128)(2,1)} %all-gather.11.cloned.1.call-done, s32[1024]{0:T(1024)S(1)} %pad_clamp_fusion), kind=kCustom, calls=%fused_computation.7.clone | custom fusion | bytes 4194336 | tf_op jit(solution)/shard_map/jit(_take)/gather | solution.py:71
  447.8 6.6 %broadcast_select_fusion = (bf16[8,4,2,4,32,128]{5,4,3,2,1,0:T(8,128)(2,1)}, bf16[8,4,2,4,32,128]{5,4,3,2,1,0:T(8,128)(2,1)}, bf16[8,4,2,4,32,128]{5,4,3,2,1,0:T(8,128)(2,1)}, bf16[8,4,2,4,32,128]{5,4,3,2,1,0:T(8,128)(2,1)}) fusion(bf16[8,4,2,4,32,128]{5,4,3,2,1,0:T(8,128)(2,1)} %gather_fusion.7, pred[8]{0:T(512)(128)(4,1)S(1)} %get-tuple-element.44, ...), kind=kLoop, calls=%fused_computation.65 | loop fusion | flops 4194304 | bytes 16777224 | tf_op jit(solution)/shard_map/jit(_take)/select_n | solution.py:71
  454.4 7.0 %fusion = bf16[2,2,128,128,32]{2,3,1,4,0:T(8,128)(2,1)S(1)} fusion(bf16[2,1,4,4,2,4,32,128]{7,5,3,4,2,1,6,0:T(4,128)(2,1)} %maximum_bitcast_fusion.1, bf16[2,1,4,4,2,4,32,128]{7,5,3,4,2,1,6,0:T(4,128)(2,1)S(1)} %bitcast.166, bf16[2,4,4,2,4,32,128,1]{6,5,4,3,1,2,0,7:T(8,128)(2,1)} %bitcast.170), kind=kOutput, calls=%fused_computation.12 | convolution fusion | flops 547356672 | bytes 10485760 | tf_op jit(solution)/shard_map/sgtkwfa,spgtkwfb->spabf/dot_general | solution.py:79
  461.4 6.7 %dynamic_update_slice.12 = bf16[2,2,128,128,128]{2,3,1,4,0:T(8,128)(2,1)} pad(bf16[2,2,128,128,32]{2,3,1,4,0:T(8,128)(2,1)S(1)} %fusion, bf16[]{:T(256)} %constant.52.clone.1), padding=0_0x0_0x0_0x0_0x0_96 | pad | bytes 20971522 | tf_op jit(solution)/shard_map/dynamic_update_slice | solution.py:82
  468.0 9.1 %fusion.2 = bf16[2,2,128,128,128]{2,3,1,4,0:T(8,128)(2,1)} fusion(bf16[2,2,128,128,128]{2,3,1,4,0:T(8,128)(2,1)} %dynamic_update_slice.12, bf16[2,1,4,4,2,4,32,128]{7,5,3,4,2,1,6,0:T(4,128)(2,1)} %maximum_bitcast_fusion.2, bf16[2,1,4,4,2,4,32,128]{7,5,3,4,2,1,6,0:T(4,128)(2,1)S(1)} %bitcast.164, bf16[2,4,4,2,4,32,128,1]{6,5,4,3,1,2,0,7:T(8,128)(2,1)} %bitcast.169), kind=kOutput, calls=%fused_computation.14 | convolution fusion | flops 547356672 | bytes 10485760 | tf_op jit(solution)/shard_map/sgtkwfa,spgtkwfb->spabf/dot_general | solution.py:79
  477.1 9.1 %fusion.4 = bf16[2,2,128,128,128]{2,3,1,4,0:T(8,128)(2,1)} fusion(bf16[2,2,128,128,128]{2,3,1,4,0:T(8,128)(2,1)} %fusion.2, bf16[2,1,4,4,2,4,32,128]{7,5,3,4,2,1,6,0:T(4,128)(2,1)} %maximum_bitcast_fusion.3, bf16[2,1,4,4,2,4,32,128]{7,5,3,4,2,1,6,0:T(4,128)(2,1)S(1)} %bitcast.162, bf16[2,4,4,2,4,32,128,1]{6,5,4,3,1,2,0,7:T(8,128)(2,1)} %bitcast.168), kind=kOutput, calls=%fused_computation.16 | convolution fusion | flops 547356672 | bytes 10485760 | tf_op jit(solution)/shard_map/sgtkwfa,spgtkwfb->spabf/dot_general | solution.py:79
  486.2 7.4 %fusion.6 = bf16[2,2,128,128,128]{2,3,1,4,0:T(8,128)(2,1)} fusion(bf16[2,2,128,128,128]{2,3,1,4,0:T(8,128)(2,1)} %fusion.4, bf16[2,1,4,4,2,4,32,128]{7,5,3,4,2,1,6,0:T(4,128)(2,1)} %maximum_bitcast_fusion.4, bf16[2,1,4,4,2,4,32,128]{7,5,3,4,2,1,6,0:T(4,128)(2,1)S(1)} %bitcast.160, bf16[2,4,4,2,4,32,128,1]{6,5,4,3,1,2,0,7:T(8,128)(2,1)S(1)} %bitcast.167), kind=kOutput, calls=%fused_computation.18 | convolution fusion | flops 547356672 | bytes 10485760 | tf_op jit(solution)/shard_map/sgtkwfa,spgtkwfb->spabf/dot_general | solution.py:79
  493.6 25.8 %copy.56 = bf16[2,2,128,128,128]{4,3,2,1,0:T(8,128)(2,1)} copy(bf16[2,2,128,128,128]{2,3,1,4,0:T(8,128)(2,1)} %fusion.6) | data formatting | bytes 33554432 | tf_op jit(solution)/shard_map/dynamic_update_slice | solution.py:82
  (68 shorter events, 24.8 us)
Async XLA Ops:
  6.5 156.9 %all-gather.5.cloned.1.call-start = ((), (), s32[]{:S(2)}) async-start(), calls=%async_computation.1 | async-start | bytes 17301504 | tf_op jit(solution)/shard_map/all_gather | solution.py:70
  6.5 8.2 %copy-start.11 = (f32[4,256,1024]{2,1,0:T(8,128)S(1)}, f32[4,256,1024]{2,1,0:T(8,128)}, u32[]{:S(2)}) copy-start(f32[4,256,1024]{2,1,0:T(8,128)} %param.5) | copy-start | bytes 12582916
  88.5 2.1 copy-start.9
  88.5 3.3 copy-start.10
  88.6 149.3 %all-gather.7.cloned.1.call-start = ((), (), s32[]{:S(2)}) async-start(), calls=%async_computation.2 | async-start | bytes 17301504 | tf_op jit(solution)/shard_map/all_gather | solution.py:70
  89.3 223.0 %all-gather.9.cloned.1.call-start = ((), (), s32[]{:S(2)}) async-start(), calls=%async_computation.3 | async-start | bytes 17301504 | tf_op jit(solution)/shard_map/all_gather | solution.py:70
  90.1 296.5 %all-gather.11.cloned.1.call-start = ((), (), s32[]{:S(2)}) async-start(), calls=%async_computation.4 | async-start | bytes 17301504 | tf_op jit(solution)/shard_map/all_gather | solution.py:70
  399.2 6.3 %copy-start = (bf16[4,2,4,2,4,32,128]{6,4,2,3,0,5,1:T(4,128)(2,1)}, bf16[4,2,4,2,4,32,128]{6,4,2,3,0,5,1:T(4,128)(2,1)S(1)}, u32[]{:S(2)}) copy-start(bf16[4,2,4,2,4,32,128]{6,4,2,3,0,5,1:T(4,128)(2,1)S(1)} %copy.103) | copy-start | bytes 6291460
  400.3 4.4 copy-start.4
  401.4 2.5 copy-start.2
  402.5 1.4 copy-start.6
  447.8 6.6 %copy-start.7 = (bf16[4,2,4,2,4,32,128]{6,4,2,3,0,5,1:T(4,128)(2,1)S(1)}, bf16[4,2,4,2,4,32,128]{6,4,2,3,0,5,1:T(4,128)(2,1)}, u32[]{:S(2)}) copy-start(bf16[4,2,4,2,4,32,128]{6,4,2,3,0,5,1:T(4,128)(2,1)} %copy-done.6) | copy-start | bytes 6291460
  461.3 6.7 %copy-start.5 = (bf16[4,2,4,2,4,32,128]{6,4,2,3,0,5,1:T(4,128)(2,1)S(1)}, bf16[4,2,4,2,4,32,128]{6,4,2,3,0,5,1:T(4,128)(2,1)}, u32[]{:S(2)}) copy-start(bf16[4,2,4,2,4,32,128]{6,4,2,3,0,5,1:T(4,128)(2,1)} %copy-done.4) | copy-start | bytes 6291460
  468.0 9.1 %copy-start.3 = (bf16[4,2,4,2,4,32,128]{6,4,2,3,0,5,1:T(4,128)(2,1)S(1)}, bf16[4,2,4,2,4,32,128]{6,4,2,3,0,5,1:T(4,128)(2,1)}, u32[]{:S(2)}) copy-start(bf16[4,2,4,2,4,32,128]{6,4,2,3,0,5,1:T(4,128)(2,1)} %copy-done.2) | copy-start | bytes 6291460
  477.1 9.1 %copy-start.1 = (bf16[4,2,4,2,4,32,128]{6,4,2,3,0,5,1:T(4,128)(2,1)S(1)}, bf16[4,2,4,2,4,32,128]{6,4,2,3,0,5,1:T(4,128)(2,1)}, u32[]{:S(2)}) copy-start(bf16[4,2,4,2,4,32,128]{6,4,2,3,0,5,1:T(4,128)(2,1)} %copy-done) | copy-start | bytes 6291460
  477.1 9.1 %copy-start.8 = (bf16[8,4,2,4,32,128]{5,4,3,2,1,0:T(8,128)(2,1)S(1)}, bf16[8,4,2,4,32,128]{5,4,3,2,1,0:T(8,128)(2,1)}, u32[]{:S(2)}) copy-start(bf16[8,4,2,4,32,128]{5,4,3,2,1,0:T(8,128)(2,1)} %get-tuple-element.32) | copy-start | bytes 6291460
Sparse Core Ops, SparseCore 0:
  88.7 74.7 all-gather.4
  165.8 72.0 all-gather.6
  240.2 72.0 all-gather.8
  314.5 72.0 all-gather.10

commit v2 on v1

--- a/solution.py
+++ b/solution.py
@@ -6,33 +6,34 @@
 SUB = 64
 BLOCK = 128
 SLOTS = 2
-CHUNKS = 4
+CHUNKS = 8
 
 
 whiten_eps = 1e-05
 
 
 def dft_table(samples, bin_count):
-    sample_ids = lax.broadcasted_iota(jnp.int32, (samples, bin_count), 0)
-    bin_ids = lax.broadcasted_iota(jnp.int32, (samples, bin_count), 1)
+    bin_ids = lax.broadcasted_iota(jnp.int32, (bin_count, samples), 0)
+    sample_ids = lax.broadcasted_iota(jnp.int32, (bin_count, samples), 1)
     phase_angle = (sample_ids * bin_ids % samples).astype(jnp.float32) * (2.0 * jnp.pi / samples)
-    return jnp.concatenate([jnp.cos(phase_angle), -jnp.sin(phase_angle)], axis=1)
+    return jnp.concatenate([jnp.cos(phase_angle), -jnp.sin(phase_angle)], axis=0)
 
 
 def whiten(flat_traces, bin_count):
     row_count, samples = flat_traces.shape
-    spectra = jnp.dot(
+    spectra = lax.dot_general(
+        dft_table(samples, bin_count),
         flat_traces,
-        dft_table(samples, bin_count),
+        (((1,), (1,)), ((), ())),
         precision=lax.Precision.HIGHEST,
         preferred_element_type=jnp.float32,
     )
-    real_band = spectra[:, :bin_count].reshape(row_count, bin_count // SUB, SUB)
-    imag_band = spectra[:, bin_count:].reshape(row_count, bin_count // SUB, SUB)
-    band_power = jnp.mean(real_band * real_band + imag_band * imag_band, axis=-1, keepdims=True)
+    real_band = spectra[:bin_count].reshape(bin_count // SUB, SUB, row_count)
+    imag_band = spectra[bin_count:].reshape(bin_count // SUB, SUB, row_count)
+    band_power = jnp.mean(real_band * real_band + imag_band * imag_band, axis=1, keepdims=True)
     factor = lax.rsqrt(band_power + whiten_eps)
-    stacked = jnp.stack([real_band * factor, imag_band * factor], axis=1)
-    return stacked.reshape(row_count, 2, bin_count).astype(jnp.bfloat16)
+    stacked = jnp.stack([real_band * factor, imag_band * factor], axis=0)
+    return stacked.reshape(2, bin_count, row_count).astype(jnp.bfloat16)
 
 
 def slot_blocks(pair_list, pair_owner, slot_ids, per_slot):
@@ -56,17 +57,18 @@
     chunk = band_bins // CHUNKS
 
     whitened = whiten(traces.reshape(win_local * chan_local, samples), bin_count)
-    whitened = whitened.reshape(win_local, per_device, BLOCK, 2, bands, band_bins)
-    whitened = jnp.transpose(whitened, (4, 1, 3, 0, 5, 2))
+    whitened = whitened.reshape(2, bands, band_bins, win_local, per_device, BLOCK)
+    whitened = jnp.transpose(whitened, (1, 4, 0, 3, 2, 5))
     relaid = lax.all_to_all(whitened, "band", split_axis=0, concat_axis=0, tiled=True)
 
     device_index = lax.axis_index("pair")
     slot_ids = device_index * SLOTS + jnp.arange(SLOTS, dtype=jnp.int32)
     first, second = slot_blocks(pair_list, pair_owner, slot_ids, per_slot)
 
+    pieces = [relaid[:, :, :, :, part * chunk:(part + 1) * chunk, :] for part in range(CHUNKS)]
     out = jnp.zeros((SLOTS, 2, BLOCK, BLOCK, band_bins), jnp.bfloat16)
     for part in range(CHUNKS):
-        piece = relaid[:, :, :, :, part * chunk:(part + 1) * chunk, :]
+        piece = pieces[part]
         gathered = lax.all_gather(piece, "pair", axis=1, tiled=True)
         left = jnp.take(gathered, first.reshape(-1), axis=1)
         left = left.reshape(left.shape[0], SLOTS, per_slot, *left.shape[2:])
@@ -79,7 +81,10 @@
         product = jnp.einsum(
             "sgtkwfa,spgtkwfb->spabf", left, paired, preferred_element_type=jnp.float32
         )
-        out = lax.dynamic_update_slice_in_dim(out, product.astype(jnp.bfloat16), part * chunk, axis=4)
+        product = product.astype(jnp.bfloat16)
+        if part + 2 < CHUNKS:
+            pieces[part + 2], product = lax.optimization_barrier((pieces[part + 2], product))
+        out = lax.dynamic_update_slice_in_dim(out, product, part * chunk, axis=4)
     return out
 
 

time: 534 us -> 624 us (1.17)
  waiting for transfers between devices: 274 us -> 377 us
  matrix products: 71.1 us -> 41.9 us
  local copies, waits for them, and re-layouts: 102 us -> 121 us
    all_gather x4 -> x8, waiting for transfers between devices: 272 us -> 376 us  [shards(): gathered = lax.all_gather(piece, 'pair', axis=1, tiled=True)]
    dot_general x1, matrix products: 38.6 us -> 14.4 us  [whiten(): lax.dot_general(dft_table(samples, bin_count), flat_traces, (((1,), (1,))...]
    dynamic_update_slice x2 -> x7, local copies, waits for them, and re-layouts: 32.5 us -> 40.7 us  [shards(): out = lax.dynamic_update_slice_in_dim(out, product, part * chunk, axis=4)]
    dot_general x4 -> x8, matrix products: 32.5 us -> 27.4 us  [shards(): jnp.einsum('sgtkwfa,spgtkwfb->spabf', left, paired, preferred_element_typ...]
    gather x4 -> x8, local copies, waits for them, and re-layouts: 30.5 us -> 33 us  [shards(): left = jnp.take(gathered, first.reshape(-1), axis=1)]
    gather x4 -> x8, local copies, waits for them, and re-layouts: 30.5 us -> 33 us  [shards(): right = jnp.take(gathered, second.reshape(-1), axis=1)]
  transfers between devices with their start and end apart: 4 -> 8, of which waited for: 4 -> 8; matrix products, arithmetic and copies ran while one was open for 5% -> 8% of each run, Pallas kernels for 0% -> 0%
where the time goes in v2:
time: 624 us; the launch traced here: 615 us
  waiting for transfers between devices  377 us (60%)
  local copies, waits for them, and re-layouts  121 us (19%)
  matrix products  41.9 us (7%)
  blocking collectives  30.1 us (5%)
  other arithmetic  29.6 us (5%)
  between operations  14.6 us (2%)
    all_gather x8, waiting for transfers between devices, shards(): gathered = lax.all_gather(piece, 'pair', axis=1, tiled=True)  376 us
    dynamic_update_slice x7, local copies, waits for them, and re-layouts, shards(): out = lax.dynamic_update_slice_in_dim(out, product, part * chunk, axis=4)  40.7 us
    gather x8, local copies, waits for them, and re-layouts, shards(): left = jnp.take(gathered, first.reshape(-1), axis=1)  33 us
    gather x8, local copies, waits for them, and re-layouts, shards(): right = jnp.take(gathered, second.reshape(-1), axis=1)  33 us
    all_to_all x1, blocking collectives, shards(): lax.all_to_all(whitened, 'band', split_axis=0, concat_axis=0, tiled=True)  30.1 us
    dot_general x8, matrix products, shards(): jnp.einsum('sgtkwfa,spgtkwfb->spabf', left, paired, preferred_element_typ...  27.4 us
    dot_general x1, matrix products, whiten(): lax.dot_general(dft_table(samples, bin_count), flat_traces, (((1,), (1,))...  14.4 us
  transfers between devices with their start and end apart: 8, of which 8 were waited for; matrix products, arithmetic and copies ran while one was open for 8% of the time, Pallas kernels for 0%

profile of v2, /device:TPU:1, one launch (start us, length us, event | category | flops | bytes accessed | tf_op | source)
XLA Modules:
  0.0 614.5 jit_solution(1269818730203177782)
XLA Ops:
  6.5 8.2 %sine_negate_fusion = (f32[512,1024]{1,0:T(8,128)S(1)}, f32[512,1024]{1,0:T(8,128)S(1)}) fusion(), kind=kLoop, calls=%fused_computation.67 | loop fusion | flops 7864320 | bytes 4194304 | tf_op jit(solution)/shard_map/neg | solution.py:19
  14.8 14.4 %fusion = f32[1024,1024]{1,0:T(8,128)S(1)} fusion(f32[1024,1024]{1,0:T(8,128)S(1)} %bitcast.286, f32[512,1024]{1,0:T(8,128)S(1)} %get-tuple-element.84, f32[512,1024]{1,0:T(8,128)S(1)} %get-tuple-element.85), kind=kOutput, calls=%fused_computation.16 | convolution fusion | flops 12885950464 | bytes 12582912 | tf_op jit(solution)/shard_map/dot_general | solution.py:24
  32.8 30.1 %all_to_all.5 = bf16[4,2,2,4,128,128]{5,4,3,2,1,0:T(8,128)(2,1)S(1)} all-to-all(bf16[4,2,2,4,128,128]{5,4,3,2,1,0:T(8,128)(2,1)S(1)} %maximum_bitcast_fusion), channel_id=1, replica_groups=mesh['band'=4,'pair'=32] {'band'}, dimensions={0} | all-to-all | bytes 4194304 | tf_op jit(solution)/shard_map/all_to_all | solution.py:62
  66.2 53.4 %all-gather.11.cloned.1.call-done = bf16[4,64,2,4,16,128]{5,4,3,2,1,0:T(8,128)(2,1)} async-done(((bf16[4,2,2,4,16,128]{5,4,3,2,1,0:T(8,128)(2,1)}), bf16[4,64,2,4,16,128]{5,4,3,2,1,0:T(8,128)(2,1)}) %all-gather.11.cloned.1.call-update) | async-done | bytes 8388624 | tf_op jit(solution)/shard_map/all_gather | solution.py:72
  125.6 4.1 gather_fusion.3
  134.1 51.7 %all-gather.15.cloned.1.call-done = bf16[4,64,2,4,16,128]{5,4,3,2,1,0:T(8,128)(2,1)} async-done(((bf16[4,2,2,4,16,128]{5,4,3,2,1,0:T(8,128)(2,1)}), bf16[4,64,2,4,16,128]{5,4,3,2,1,0:T(8,128)(2,1)}) %all-gather.15.cloned.1.call-update) | async-done | bytes 8388624 | tf_op jit(solution)/shard_map/all_gather | solution.py:72
  185.8 4.1 gather_fusion.6
  190.7 4.1 gather_fusion.7
  199.5 41.0 %all-gather.9.cloned.1.call-done = bf16[4,64,2,4,16,128]{5,4,3,2,1,0:T(8,128)(2,1)} async-done(((bf16[4,2,2,4,16,128]{5,4,3,2,1,0:T(8,128)(2,1)}), bf16[4,64,2,4,16,128]{5,4,3,2,1,0:T(8,128)(2,1)}) %all-gather.9.cloned.1.call-update) | async-done | bytes 8388624 | tf_op jit(solution)/shard_map/all_gather | solution.py:72
  240.5 4.1 gather_fusion
  244.7 4.1 gather_fusion.1
  248.8 46.3 %all-gather.19.cloned.1.call-done = bf16[4,64,2,4,16,128]{5,4,3,2,1,0:T(8,128)(2,1)} async-done(((bf16[4,2,2,4,16,128]{5,4,3,2,1,0:T(8,128)(2,1)}), bf16[4,64,2,4,16,128]{5,4,3,2,1,0:T(8,128)(2,1)}) %all-gather.19.cloned.1.call-update) | async-done | bytes 8388624 | tf_op jit(solution)/shard_map/all_gather | solution.py:72
  302.4 4.1 gather_fusion.11
  317.4 47.2 %all-gather.23.cloned.1.call-done = bf16[4,64,2,4,16,128]{5,4,3,2,1,0:T(8,128)(2,1)} async-done(((bf16[4,2,2,4,16,128]{5,4,3,2,1,0:T(8,128)(2,1)}), bf16[4,64,2,4,16,128]{5,4,3,2,1,0:T(8,128)(2,1)}) %all-gather.23.cloned.1.call-update) | async-done | bytes 8388624 | tf_op jit(solution)/shard_map/all_gather | solution.py:72
  364.6 4.1 gather_fusion.14
  368.7 50.4 %all-gather.13.cloned.1.call-done = bf16[4,64,2,4,16,128]{5,4,3,2,1,0:T(8,128)(2,1)} async-done(((bf16[4,2,2,4,16,128]{5,4,3,2,1,0:T(8,128)(2,1)}), bf16[4,64,2,4,16,128]{5,4,3,2,1,0:T(8,128)(2,1)}) %all-gather.13.cloned.1.call-update) | async-done | bytes 8388624 | tf_op jit(solution)/shard_map/all_gather | solution.py:72
  419.2 4.1 gather_fusion.4
  430.9 4.1 gather_fusion.5
  440.5 52.5 %all-gather.17.cloned.1.call-done = bf16[4,64,2,4,16,128]{5,4,3,2,1,0:T(8,128)(2,1)} async-done(((bf16[4,2,2,4,16,128]{5,4,3,2,1,0:T(8,128)(2,1)}), bf16[4,64,2,4,16,128]{5,4,3,2,1,0:T(8,128)(2,1)}) %all-gather.17.cloned.1.call-update) | async-done | bytes 8388624 | tf_op jit(solution)/shard_map/all_gather | solution.py:72
  492.9 4.1 gather_fusion.8
  500.2 4.1 gather_fusion.9
  509.9 6.5 %dynamic_update_slice.24 = bf16[2,2,128,128,128]{2,3,1,4,0:T(8,128)(2,1)} pad(bf16[2,2,128,128,16]{2,3,1,4,0:T(8,128)(2,1)S(1)} %copy-done.16, bf16[]{:T(256)} %constant.56.clone.1), padding=0_0x0_0x0_0x0_0x0_112 | pad | bytes 18874370 | tf_op jit(solution)/shard_map/dynamic_update_slice | solution.py:87
  529.0 33.4 %all-gather.21.cloned.1.call-done = bf16[4,64,2,4,16,128]{5,4,3,2,1,0:T(8,128)(2,1)} async-done(((bf16[4,2,2,4,16,128]{5,4,3,2,1,0:T(8,128)(2,1)}), bf16[4,64,2,4,16,128]{5,4,3,2,1,0:T(8,128)(2,1)}) %all-gather.21.cloned.1.call-update) | async-done | bytes 8388624 | tf_op jit(solution)/shard_map/all_gather | solution.py:72
  581.4 25.8 %copy.100 = bf16[2,2,128,128,128]{4,3,2,1,0:T(8,128)(2,1)} copy(bf16[2,2,128,128,128]{2,3,1,4,0:T(8,128)(2,1)} %bitcast_dynamic-update-slice_fusion) | data formatting | bytes 33554432 | tf_op jit(solution)/shard_map/dynamic_update_slice | solution.py:87
  (143 shorter events, 93.5 us)
Async XLA Ops:
  6.5 113.1 %all-gather.11.cloned.1.call-start = ((), (), s32[]{:S(2)}) async-start(), calls=%async_computation.2 | async-start | bytes 8650752 | tf_op jit(solution)/shard_map/all_gather | solution.py:72
  6.5 8.2 %copy-start.23 = (f32[4,256,1024]{2,1,0:T(8,128)S(1)}, f32[4,256,1024]{2,1,0:T(8,128)}, u32[]{:S(2)}) copy-start(f32[4,256,1024]{2,1,0:T(8,128)} %param.5) | copy-start | bytes 12582916
  62.9 1.6 copy-start.21
  62.9 2.9 copy-start.22
  64.5 121.3 %all-gather.15.cloned.1.call-start = ((), (), s32[]{:S(2)}) async-start(), calls=%async_computation.4 | async-start | bytes 8650752 | tf_op jit(solution)/shard_map/all_gather | solution.py:72
  133.3 107.2 %all-gather.9.cloned.1.call-start = ((), (), s32[]{:S(2)}) async-start(), calls=%async_computation.1 | async-start | bytes 8650752 | tf_op jit(solution)/shard_map/all_gather | solution.py:72
  134.0 161.1 %all-gather.19.cloned.1.call-start = ((), (), s32[]{:S(2)}) async-start(), calls=%async_computation.6 | async-start | bytes 8650752 | tf_op jit(solution)/shard_map/all_gather | solution.py:72
  199.4 165.1 %all-gather.23.cloned.1.call-start = ((), (), s32[]{:S(2)}) async-start(), calls=%async_computation.8 | async-start | bytes 8650752 | tf_op jit(solution)/shard_map/all_gather | solution.py:72
  306.5 1.2 copy-start.10
  308.5 3.7 copy-start
  312.1 107.1 %all-gather.13.cloned.1.call-start = ((), (), s32[]{:S(2)}) async-start(), calls=%async_computation.3 | async-start | bytes 8650752 | tf_op jit(solution)/shard_map/all_gather | solution.py:72
  317.3 175.6 %all-gather.17.cloned.1.call-start = ((), (), s32[]{:S(2)}) async-start(), calls=%async_computation.5 | async-start | bytes 8650752 | tf_op jit(solution)/shard_map/all_gather | solution.py:72
  435.1 1.3 copy-start.2
  435.1 1.9 copy-start.20
  440.4 122.0 %all-gather.21.cloned.1.call-start = ((), (), s32[]{:S(2)}) async-start(), calls=%async_computation.7 | async-start | bytes 8650752 | tf_op jit(solution)/shard_map/all_gather | solution.py:72
  504.3 1.9 copy-start.4
  506.2 3.7 copy-start.16
  509.9 6.5 %copy-start.5 = (bf16[2,2,128,128,16]{2,3,1,4,0:T(8,128)(2,1)S(1)}, bf16[2,2,128,128,16]{2,3,1,4,0:T(8,128)(2,1)}, u32[]{:S(2)}) copy-start(bf16[2,2,128,128,16]{2,3,1,4,0:T(8,128)(2,1)} %fusion.39) | copy-start | bytes 6291460
  518.6 2.1 copy-start.8
  520.7 2.2 copy-start.6
  522.9 2.2 copy-start.9
  525.1 2.2 copy-start.7
  574.6 3.4 copy-start.17
  574.7 3.4 copy-start.19
  (8 other events, 8.9 us)
Sparse Core Ops, SparseCore 0:
  64.6 54.9 all-gather.10
  133.4 52.3 all-gather.14
  188.1 52.3 all-gather.8
  242.7 52.3 all-gather.18
  312.2 52.3 all-gather.22
  366.8 52.3 all-gather.12
  440.5 52.3 all-gather.16
  510.0 52.3 all-gather.20

commit v3 on v2

--- a/solution.py
+++ b/solution.py
@@ -2,11 +2,12 @@
 import jax.numpy as jnp
 from jax import lax
 from jax.sharding import PartitionSpec as P
+from jax.experimental.layout import Layout, with_layout_constraint
 
 SUB = 64
 BLOCK = 128
 SLOTS = 2
-CHUNKS = 8
+CHUNKS = 4
 
 
 whiten_eps = 1e-05
@@ -65,23 +66,24 @@
     slot_ids = device_index * SLOTS + jnp.arange(SLOTS, dtype=jnp.int32)
     first, second = slot_blocks(pair_list, pair_owner, slot_ids, per_slot)
 
-    pieces = [relaid[:, :, :, :, part * chunk:(part + 1) * chunk, :] for part in range(CHUNKS)]
+    pieces = [
+        jnp.transpose(relaid[:, :, :, :, part * chunk:(part + 1) * chunk, :], (1, 0, 2, 3, 4, 5))
+        for part in range(CHUNKS)
+    ]
     out = jnp.zeros((SLOTS, 2, BLOCK, BLOCK, band_bins), jnp.bfloat16)
     for part in range(CHUNKS):
         piece = pieces[part]
-        gathered = lax.all_gather(piece, "pair", axis=1, tiled=True)
-        left = jnp.take(gathered, first.reshape(-1), axis=1)
-        left = left.reshape(left.shape[0], SLOTS, per_slot, *left.shape[2:])
-        left = jnp.moveaxis(left, 1, 0)
-        right = jnp.take(gathered, second.reshape(-1), axis=1)
-        right = right.reshape(right.shape[0], SLOTS, per_slot, *right.shape[2:])
-        right = jnp.moveaxis(right, 1, 0)
+        gathered = lax.all_gather(piece, "pair", axis=0, tiled=True)
+        left = jnp.take(gathered, first.reshape(-1), axis=0)
+        left = left.reshape(SLOTS, per_slot, *left.shape[1:])
+        right = jnp.take(gathered, second.reshape(-1), axis=0)
+        right = right.reshape(SLOTS, per_slot, *right.shape[1:])
         rotated = jnp.stack([-right[:, :, :, 1], right[:, :, :, 0]], axis=3)
         paired = jnp.stack([right, rotated], axis=1)
         product = jnp.einsum(
-            "sgtkwfa,spgtkwfb->spabf", left, paired, preferred_element_type=jnp.float32
+            "stgkwfa,sptgkwfb->spabf", left, paired, preferred_element_type=jnp.float32
         )
-        product = product.astype(jnp.bfloat16)
+        product = with_layout_constraint(product.astype(jnp.bfloat16), Layout((0, 1, 2, 3, 4)))
         if part + 2 < CHUNKS:
             pieces[part + 2], product = lax.optimization_barrier((pieces[part + 2], product))
         out = lax.dynamic_update_slice_in_dim(out, product, part * chunk, axis=4)

time: 624 us -> 1110 us (1.78)
  local copies, waits for them, and re-layouts: 121 us -> 825 us
  waiting for transfers between devices: 377 us -> 139 us
    dynamic_update_slice x7 -> x4, local copies, waits for them, and re-layouts: 40.7 us -> 619 us  [shards(): out = lax.dynamic_update_slice_in_dim(out, product, part * chunk, axis=4)]
    all_gather x8 -> x4, waiting for transfers between devices: 376 us -> 139 us  [shards(): gathered = lax.all_gather(piece, 'pair', axis=0, tiled=True)]
    convert_element_type x0 -> x4, local copies, waits for them, and re-layouts: none -> 114 us  [shards(): product.astype(jnp.bfloat16)]
    dot_general x8 -> x4, matrix products: 27.4 us -> 36.8 us  [shards(): jnp.einsum('stgkwfa,sptgkwfb->spabf', left, paired, preferred_element_typ...]
    gather x16 -> x8, local copies, waits for them, and re-layouts: 66.1 us -> 63.3 us  [the longest x4 31.6 us: shards(): right = jnp.take(gathered, second.reshape(-1), axis=0)]
  transfers between devices with their start and end apart: 8 -> 4, of which waited for: 8 -> 2; matrix products, arithmetic and copies ran while one was open for 8% -> 25% of each run, Pallas kernels for 0% -> 0%
where the time goes in v3:
time: 1110 us; the launch traced here: 1090 us
  local copies, waits for them, and re-layouts  825 us (74%)
  waiting for transfers between devices  139 us (13%)
  matrix products  51 us (5%)
  other arithmetic  36.1 us (3%)
  blocking collectives  30.1 us (3%)
  between operations  13.6 us (1%)
    dynamic_update_slice x4, local copies, waits for them, and re-layouts, shards(): out = lax.dynamic_update_slice_in_dim(out, product, part * chunk, axis=4)  619 us
    all_gather x4, waiting for transfers between devices, shards(): gathered = lax.all_gather(piece, 'pair', axis=0, tiled=True)  139 us
    convert_element_type x4, local copies, waits for them, and re-layouts, shards(): product.astype(jnp.bfloat16)  114 us
    dot_general x4, matrix products, shards(): jnp.einsum('stgkwfa,sptgkwfb->spabf', left, paired, preferred_element_typ...  36.8 us
    gather x4, local copies, waits for them, and re-layouts, shards(): right = jnp.take(gathered, second.reshape(-1), axis=0)  31.6 us
    gather x4, local copies, waits for them, and re-layouts, shards(): left = jnp.take(gathered, first.reshape(-1), axis=0)  31.6 us
    all_to_all x1, blocking collectives, shards(): lax.all_to_all(whitened, 'band', split_axis=0, concat_axis=0, tiled=True)  30.1 us
  transfers between devices with their start and end apart: 4, of which 2 were waited for; matrix products, arithmetic and copies ran while one was open for 25% of the time, Pallas kernels for 0%

profile of v3, /device:TPU:1, one launch (start us, length us, event | category | flops | bytes accessed | tf_op | source)
XLA Modules:
  0.0 1094.9 jit_solution(4734999059504382016)
XLA Ops:
  6.5 8.2 sine_negate_fusion
  14.8 14.2 %fusion = f32[1024,1024]{1,0:T(8,128)S(1)} fusion(f32[1024,1024]{1,0:T(8,128)S(1)} %bitcast.102, f32[512,1024]{1,0:T(8,128)S(1)} %get-tuple-element.40, f32[512,1024]{1,0:T(8,128)S(1)} %get-tuple-element.41), kind=kOutput, calls=%fused_computation.12 | convolution fusion | flops 12885950464 | bytes 12582912 | tf_op jit(solution)/shard_map/dot_general | solution.py:25
  30.2 10.6 stack.50
  42.3 30.1 %all_to_all.5 = bf16[4,2,2,4,128,128]{5,4,3,2,1,0:T(8,128)(2,1)S(1)} all-to-all(bf16[4,2,2,4,128,128]{5,4,3,2,1,0:T(8,128)(2,1)S(1)} %maximum_bitcast_fusion), channel_id=1, replica_groups=mesh['band'=4,'pair'=32] {'band'}, dimensions={0} | all-to-all | bytes 4194304 | tf_op jit(solution)/shard_map/all_to_all | solution.py:63
  76.5 72.3 %all-gather.7.cloned.1.call-done = bf16[64,4,2,4,32,128]{5,4,3,2,1,0:T(8,128)(2,1)} async-done(((bf16[2,4,2,4,32,128]{5,4,3,2,1,0:T(8,128)(2,1)}), bf16[64,4,2,4,32,128]{5,4,3,2,1,0:T(8,128)(2,1)}) %all-gather.7.cloned.1.call-update) | async-done | bytes 16777232 | tf_op jit(solution)/shard_map/all_gather | solution.py:76
  148.8 7.9 gather_fusion.2
  156.7 66.5 %all-gather.5.cloned.1.call-done = bf16[64,4,2,4,32,128]{5,4,3,2,1,0:T(8,128)(2,1)} async-done(((bf16[2,4,2,4,32,128]{5,4,3,2,1,0:T(8,128)(2,1)}), bf16[64,4,2,4,32,128]{5,4,3,2,1,0:T(8,128)(2,1)}) %all-gather.5.cloned.1.call-update) | async-done | bytes 16777232 | tf_op jit(solution)/shard_map/all_gather | solution.py:76
  223.2 7.9 gather_fusion
  240.4 7.9 gather_fusion.3
  248.3 7.9 gather_fusion.1
  261.0 12.0 %bitcast_convert_fusion.2 = bf16[2,32,2,128,128]{4,3,2,1,0:T(8,128)(2,1)} fusion(bf16[2,1,4,4,2,4,32,128]{7,5,2,4,3,1,6,0:T(4,128)(2,1)S(1)} %copy-done.3, bf16[2,1,4,4,2,4,32,128]{7,5,2,4,3,1,6,0:T(4,128)(2,1)S(1)} %copy-done.2, bf16[2,4,4,2,4,32,128,1]{6,5,4,3,2,1,0,7:T(8,128)(2,1)} %bitcast.96), kind=kOutput, calls=%fused_computation.10 | convolution fusion | flops 547356672 | bytes 10485760 | tf_op jit(solution)/shard_map/stgkwfa,sptgkwfb->spabf/dot_general | solution.py:83
  273.0 28.6 %copy.98 = bf16[2,32,2,128,128]{1,3,4,2,0:T(8,128)(2,1)} copy(bf16[2,32,2,128,128]{4,3,2,1,0:T(8,128)(2,1)} %bitcast_convert_fusion.2) | data formatting | bytes 8388608 | tf_op jit(solution)/shard_map/convert_element_type | solution.py:86
  313.5 28.6 %copy.92 = bf16[2,32,2,128,128]{1,3,4,2,0:T(8,128)(2,1)} copy(bf16[2,32,2,128,128]{4,3,2,1,0:T(8,128)(2,1)} %bitcast_convert_fusion.3) | data formatting | bytes 8388608 | tf_op jit(solution)/shard_map/convert_element_type | solution.py:86
  342.9 16.2 %dynamic_update_slice.12 = bf16[2,2,128,128,128]{4,3,2,1,0:T(8,128)(2,1)} pad(bf16[2,2,128,128,32]{4,3,2,1,0:T(8,128)(2,1)} %bitcast.84, bf16[]{:T(256)} %constant.52.clone.1), padding=0_0x0_0x0_0x0_0x0_96 | pad | bytes 20971522 | tf_op jit(solution)/shard_map/dynamic_update_slice | solution.py:89
  359.1 201.6 %dynamic_update_slice.13 = bf16[2,2,128,128,128]{4,3,2,1,0:T(8,128)(2,1)} dynamic-update-slice(bf16[2,2,128,128,128]{4,3,2,1,0:T(8,128)(2,1)} %dynamic_update_slice.12, bf16[2,2,128,128,32]{4,3,2,1,0:T(8,128)(2,1)} %bitcast.81, s32[]{:T(128)} %constant.22.clone.1, s32[]{:T(128)} %constant.22.clone.1, s32[]{:T(128)} %constant.22.clone.1, s32[]{:T(128)} %constant.22.clone.1, s32[]{:T(128)} %constant.53.clone.1) | dynamic-update-slice | bytes 8388612 | tf_op jit(solution)/shard_map/dynamic_update_slice | solution.py:89
  560.7 7.9 gather_fusion.6
  568.6 8.0 gather_fusion.4
  585.9 7.9 gather_fusion.7
  593.8 7.9 gather_fusion.5
  606.5 12.3 %bitcast_convert_fusion.1 = bf16[2,32,2,128,128]{4,3,2,1,0:T(8,128)(2,1)} fusion(bf16[2,1,4,4,2,4,32,128]{7,5,2,4,3,1,6,0:T(4,128)(2,1)S(1)} %copy-done.1, bf16[2,1,4,4,2,4,32,128]{7,5,2,4,3,1,6,0:T(4,128)(2,1)S(1)} %copy-done, bf16[2,4,4,2,4,32,128,1]{6,5,4,3,2,1,0,7:T(8,128)(2,1)} %bitcast.95), kind=kOutput, calls=%fused_computation.9 | convolution fusion | flops 547356672 | bytes 10485760 | tf_op jit(solution)/shard_map/stgkwfa,sptgkwfb->spabf/dot_general | solution.py:83
  618.8 28.6 %copy.104 = bf16[2,32,2,128,128]{1,3,4,2,0:T(8,128)(2,1)} copy(bf16[2,32,2,128,128]{4,3,2,1,0:T(8,128)(2,1)} %bitcast_convert_fusion.1) | data formatting | bytes 8388608 | tf_op jit(solution)/shard_map/convert_element_type | solution.py:86
  658.0 28.6 %copy.110 = bf16[2,32,2,128,128]{1,3,4,2,0:T(8,128)(2,1)} copy(bf16[2,32,2,128,128]{4,3,2,1,0:T(8,128)(2,1)} %bitcast_convert_fusion) | data formatting | bytes 8388608 | tf_op jit(solution)/shard_map/convert_element_type | solution.py:86
  686.5 200.8 %dynamic_update_slice.14 = bf16[2,2,128,128,128]{4,3,2,1,0:T(8,128)(2,1)} dynamic-update-slice(bf16[2,2,128,128,128]{4,3,2,1,0:T(8,128)(2,1)} %dynamic_update_slice.13, bf16[2,2,128,128,32]{4,3,2,1,0:T(8,128)(2,1)} %bitcast.82, s32[]{:T(128)} %constant.22.clone.1, s32[]{:T(128)} %constant.22.clone.1, s32[]{:T(128)} %constant.22.clone.1, s32[]{:T(128)} %constant.22.clone.1, s32[]{:T(128)} %constant.54.clone.1) | dynamic-update-slice | bytes 8388612 | tf_op jit(solution)/shard_map/dynamic_update_slice | solution.py:89
  887.4 200.8 %dynamic_update_slice.15 = bf16[2,2,128,128,128]{4,3,2,1,0:T(8,128)(2,1)} dynamic-update-slice(bf16[2,2,128,128,128]{4,3,2,1,0:T(8,128)(2,1)} %dynamic_update_slice.14, bf16[2,2,128,128,32]{4,3,2,1,0:T(8,128)(2,1)} %bitcast.83, s32[]{:T(128)} %constant.22.clone.1, s32[]{:T(128)} %constant.22.clone.1, s32[]{:T(128)} %constant.22.clone.1, s32[]{:T(128)} %constant.22.clone.1, s32[]{:T(128)} %constant.55.clone.1) | dynamic-update-slice | bytes 8388612 | tf_op jit(solution)/shard_map/dynamic_update_slice | solution.py:89
  (84 shorter events, 58.0 us)
Async XLA Ops:
  6.5 142.3 %all-gather.7.cloned.1.call-start = ((), (), s32[]{:S(2)}) async-start(), calls=%async_computation.2 | async-start | bytes 17301504 | tf_op jit(solution)/shard_map/all_gather | solution.py:76
  6.5 8.2 copy-start.8
  73.0 1.9 copy-start.6
  73.0 3.1 copy-start.7
  73.8 149.3 %all-gather.5.cloned.1.call-start = ((), (), s32[]{:S(2)}) async-start(), calls=%async_computation.1 | async-start | bytes 17301504 | tf_op jit(solution)/shard_map/all_gather | solution.py:76
  74.8 485.9 %all-gather.11.cloned.1.call-start = ((), (), s32[]{:S(2)}) async-start(), calls=%async_computation.4 | async-start | bytes 17301504 | tf_op jit(solution)/shard_map/all_gather | solution.py:76
  256.2 4.8 copy-start.2
  256.2 4.8 copy-start.3
  302.4 266.2 %all-gather.9.cloned.1.call-start = ((), (), s32[]{:S(2)}) async-start(), calls=%async_computation.3 | async-start | bytes 17301504 | tf_op jit(solution)/shard_map/all_gather | solution.py:76
  305.7 1.6 copy-start.4
  601.7 4.8 copy-start
  601.7 4.8 copy-start.1
  650.1 1.6 copy-start.5
Sparse Core Ops, SparseCore 0:
  74.0 74.7 all-gather.6
  151.1 72.0 all-gather.4
  302.6 72.0 all-gather.10
  376.8 72.1 all-gather.8

commit v4 on v2

--- a/solution.py
+++ b/solution.py
@@ -6,7 +6,7 @@
 SUB = 64
 BLOCK = 128
 SLOTS = 2
-CHUNKS = 8
+CHUNKS = 4
 
 
 whiten_eps = 1e-05
@@ -59,17 +59,20 @@
     whitened = whiten(traces.reshape(win_local * chan_local, samples), bin_count)
     whitened = whitened.reshape(2, bands, band_bins, win_local, per_device, BLOCK)
     whitened = jnp.transpose(whitened, (1, 4, 0, 3, 2, 5))
-    relaid = lax.all_to_all(whitened, "band", split_axis=0, concat_axis=0, tiled=True)
 
     device_index = lax.axis_index("pair")
     slot_ids = device_index * SLOTS + jnp.arange(SLOTS, dtype=jnp.int32)
     first, second = slot_blocks(pair_list, pair_owner, slot_ids, per_slot)
 
-    pieces = [relaid[:, :, :, :, part * chunk:(part + 1) * chunk, :] for part in range(CHUNKS)]
+    pieces = [
+        lax.all_to_all(
+            whitened[:, :, :, :, part * chunk:(part + 1) * chunk, :], "band", split_axis=0, concat_axis=0, tiled=True
+        )
+        for part in range(CHUNKS)
+    ]
     out = jnp.zeros((SLOTS, 2, BLOCK, BLOCK, band_bins), jnp.bfloat16)
     for part in range(CHUNKS):
-        piece = pieces[part]
-        gathered = lax.all_gather(piece, "pair", axis=1, tiled=True)
+        gathered = lax.all_gather(pieces[part], "pair", axis=1, tiled=True)
         left = jnp.take(gathered, first.reshape(-1), axis=1)
         left = left.reshape(left.shape[0], SLOTS, per_slot, *left.shape[2:])
         left = jnp.moveaxis(left, 1, 0)

time: 624 us -> 503 us (0.81)
  waiting for transfers between devices: 377 us -> 239 us
  other arithmetic: 29.6 us -> 39.9 us
  starting transfers between devices: 0.29 us -> 7.59 us
    all_gather x8 -> x4, waiting for transfers between devices: 376 us -> 239 us  [shards(): gathered = lax.all_gather(pieces[part], 'pair', axis=1, tiled=True)]
    another operation x4, local copies, waits for them, and re-layouts: 2.17 us -> 13.2 us  [whiten(): stacked = jnp.stack([real_band * factor, imag_band * factor], axis=0)]
    all_to_all x0 -> x2, starting transfers between devices: none -> 7.5 us  [shards(): lax.all_to_all(whitened[:, :, :, :, part * chunk:(part + 1) * chunk, :],...]
    dot_general x8 -> x4, matrix products: 27.4 us -> 33.7 us  [shards(): jnp.einsum('sgtkwfa,spgtkwfb->spabf', left, paired, preferred_element_typ...]
    all_to_all x1 -> x2, blocking collectives: 30.1 us -> 24.3 us  [shards(): lax.all_to_all(whitened[:, :, :, :, part * chunk:(part + 1) * chunk, :],...]
    dynamic_update_slice x7 -> x3, local copies, waits for them, and re-layouts: 40.7 us -> 36.9 us  [shards(): out = lax.dynamic_update_slice_in_dim(out, product, part * chunk, axis=4)]
    gather x8 -> x4, local copies, waits for them, and re-layouts: 33 us -> 29.2 us  [shards(): right = jnp.take(gathered, second.reshape(-1), axis=1)]
    gather x8 -> x4, local copies, waits for them, and re-layouts: 33 us -> 31.7 us  [shards(): left = jnp.take(gathered, first.reshape(-1), axis=1)]
  transfers between devices with their start and end apart: 8 -> 6, of which waited for: 8 -> 4; matrix products, arithmetic and copies ran while one was open for 8% -> 16% of each run, Pallas kernels for 0% -> 0%
where the time goes in v4:
time: 503 us; the launch traced here: 493 us
  waiting for transfers between devices  239 us (48%)
  local copies, waits for them, and re-layouts  121 us (24%)
  matrix products  48 us (10%)
  other arithmetic  39.9 us (8%)
  blocking collectives  24.3 us (5%)
  between operations  13.8 us (3%)
  starting transfers between devices  7.59 us (2%)
    all_gather x4, waiting for transfers between devices, shards(): gathered = lax.all_gather(pieces[part], 'pair', axis=1, tiled=True)  239 us
    dynamic_update_slice x3, local copies, waits for them, and re-layouts, shards(): out = lax.dynamic_update_slice_in_dim(out, product, part * chunk, axis=4)  36.9 us
    dot_general x4, matrix products, shards(): jnp.einsum('sgtkwfa,spgtkwfb->spabf', left, paired, preferred_element_typ...  33.7 us
    gather x4, local copies, waits for them, and re-layouts, shards(): left = jnp.take(gathered, first.reshape(-1), axis=1)  31.7 us
    gather x4, local copies, waits for them, and re-layouts, shards(): right = jnp.take(gathered, second.reshape(-1), axis=1)  29.2 us
    all_to_all x2, blocking collectives, shards(): lax.all_to_all(whitened[:, :, :, :, part * chunk:(part + 1) * chunk, :],...  24.3 us
    dot_general x1, matrix products, whiten(): lax.dot_general(dft_table(samples, bin_count), flat_traces, (((1,), (1,))...  14.2 us
    another operation x4, local copies, waits for them, and re-layouts, whiten(): stacked = jnp.stack([real_band * factor, imag_band * factor], axis=0)  13.2 us
  transfers between devices with their start and end apart: 6, of which 4 were waited for; matrix products, arithmetic and copies ran while one was open for 16% of the time, Pallas kernels for 0%

profile of v4, /device:TPU:1, one launch (start us, length us, event | category | flops | bytes accessed | tf_op | source)
XLA Modules:
  0.0 493.3 jit_solution(7541066848693522159)
XLA Ops:
  6.5 8.2 %sine_negate_fusion = (f32[512,1024]{1,0:T(8,128)S(1)}, f32[512,1024]{1,0:T(8,128)S(1)}) fusion(), kind=kLoop, calls=%fused_computation.59 | loop fusion | flops 7864320 | bytes 4194304 | tf_op jit(solution)/shard_map/neg | solution.py:19
  14.8 14.2 %fusion.6 = f32[1024,1024]{1,0:T(8,128)S(1)} fusion(f32[1024,1024]{1,0:T(8,128)S(1)} %bitcast.166, f32[512,1024]{1,0:T(8,128)S(1)} %get-tuple-element.48, f32[512,1024]{1,0:T(8,128)S(1)} %get-tuple-element.49), kind=kOutput, calls=%fused_computation.18 | convolution fusion | flops 12885950464 | bytes 12582912 | tf_op jit(solution)/shard_map/dot_general | solution.py:24
  30.2 11.9 %stack.61 = bf16[1,4,128,4,2,128]{5,4,3,2,1,0:T(2,128)(2,1)S(1)} reshape(bf16[512,1024]{1,0:T(8,128)(2,1)S(1)} %get-tuple-element.16) | data formatting | bytes 2097152 | tf_op jit(solution)/shard_map/stack | solution.py:35
  45.0 13.5 %all_to_all.20 = bf16[4,2,2,4,32,128]{5,4,3,2,1,0:T(8,128)(2,1)} all-to-all(bf16[4,2,2,4,32,128]{5,4,3,2,1,0:T(8,128)(2,1)S(1)} %get-tuple-element.32), channel_id=1, replica_groups=mesh['band'=4,'pair'=32] {'band'}, dimensions={0} | all-to-all | bytes 1048576 | tf_op jit(solution)/shard_map/all_to_all | solution.py:68
  58.6 10.8 %all_to_all.21 = bf16[4,2,2,4,32,128]{5,4,3,2,1,0:T(8,128)(2,1)} all-to-all(bf16[4,2,2,4,32,128]{5,4,3,2,1,0:T(8,128)(2,1)S(1)} %get-tuple-element.30), channel_id=1, replica_groups=mesh['band'=4,'pair'=32] {'band'}, dimensions={0} | all-to-all | bytes 1048576 | tf_op jit(solution)/shard_map/all_to_all | solution.py:68
  74.7 58.8 %all-gather.5.cloned.1.call-done = bf16[4,64,2,4,32,128]{5,4,3,2,1,0:T(8,128)(2,1)} async-done(((bf16[4,2,2,4,32,128]{5,4,3,2,1,0:T(8,128)(2,1)}), bf16[4,64,2,4,32,128]{5,4,3,2,1,0:T(8,128)(2,1)}) %all-gather.5.cloned.1.call-update) | async-done | bytes 16777232 | tf_op jit(solution)/shard_map/all_gather | solution.py:75
  133.4 6.7 %gather_fusion = bf16[8,4,2,4,32,128]{5,4,3,2,1,0:T(8,128)(2,1)S(1)} fusion(bf16[4,64,2,4,32,128]{5,4,3,2,1,0:T(8,128)(2,1)} %all-gather.5.cloned.1.call-done, s32[1024]{0:T(1024)S(1)} %pad_clamp_fusion.1), kind=kCustom, calls=%fused_computation.clone | custom fusion | bytes 4194336 | tf_op jit(solution)/shard_map/jit(_take)/gather | solution.py:79
  140.2 67.7 %all-gather.7.cloned.1.call-done = bf16[4,64,2,4,32,128]{5,4,3,2,1,0:T(8,128)(2,1)} async-done(((bf16[4,2,2,4,32,128]{5,4,3,2,1,0:T(8,128)(2,1)}), bf16[4,64,2,4,32,128]{5,4,3,2,1,0:T(8,128)(2,1)}) %all-gather.7.cloned.1.call-update) | async-done | bytes 16777232 | tf_op jit(solution)/shard_map/all_gather | solution.py:75
  207.9 7.9 %gather_fusion.2 = bf16[8,4,2,4,32,128]{5,4,3,2,1,0:T(8,128)(2,1)} fusion(bf16[4,64,2,4,32,128]{5,4,3,2,1,0:T(8,128)(2,1)} %all-gather.7.cloned.1.call-done, s32[1024]{0:T(1024)S(1)} %pad_clamp_fusion.1), kind=kCustom, calls=%fused_computation.2.clone | custom fusion | bytes 4194336 | tf_op jit(solution)/shard_map/jit(_take)/gather | solution.py:79
  223.6 8.0 %gather_fusion.1 = bf16[8,4,2,4,32,128]{5,4,3,2,1,0:T(8,128)(2,1)} fusion(bf16[4,64,2,4,32,128]{5,4,3,2,1,0:T(8,128)(2,1)} %all-gather.5.cloned.1.call-done, s32[1024]{0:T(1024)S(1)} %pad_clamp_fusion), kind=kCustom, calls=%fused_computation.1.clone | custom fusion | bytes 4194336 | tf_op jit(solution)/shard_map/jit(_take)/gather | solution.py:76
  231.6 7.9 %gather_fusion.3 = bf16[8,4,2,4,32,128]{5,4,3,2,1,0:T(8,128)(2,1)} fusion(bf16[4,64,2,4,32,128]{5,4,3,2,1,0:T(8,128)(2,1)} %all-gather.7.cloned.1.call-done, s32[1024]{0:T(1024)S(1)} %pad_clamp_fusion), kind=kCustom, calls=%fused_computation.3.clone | custom fusion | bytes 4194336 | tf_op jit(solution)/shard_map/jit(_take)/gather | solution.py:76
  243.6 6.1 %fusion = bf16[2,2,128,128,32]{2,3,1,4,0:T(8,128)(2,1)} fusion(bf16[2,1,4,4,2,4,32,128]{7,5,3,4,2,1,6,0:T(4,128)(2,1)S(1)} %copy-done.6, bf16[2,1,4,4,2,4,32,128]{7,5,3,4,2,1,6,0:T(4,128)(2,1)S(1)} %bitcast.150, bf16[2,4,4,2,4,32,128,1]{6,5,4,3,1,2,0,7:T(8,128)(2,1)S(1)} %bitcast.160), kind=kOutput, calls=%fused_computation.12 | convolution fusion | flops 547356672 | bytes 10485760 | tf_op jit(solution)/shard_map/sgtkwfa,spgtkwfb->spabf/dot_general | solution.py:84
  259.7 6.3 %fusion.1 = bf16[2,2,128,128,32]{2,3,1,4,0:T(8,128)(2,1)} fusion(bf16[2,1,4,4,2,4,32,128]{7,5,3,4,2,1,6,0:T(4,128)(2,1)S(1)} %maximum_bitcast_fusion.2, bf16[2,1,4,4,2,4,32,128]{7,5,3,4,2,1,6,0:T(4,128)(2,1)S(1)} %bitcast.152, bf16[2,4,4,2,4,32,128,1]{6,5,4,3,1,2,0,7:T(8,128)(2,1)S(1)} %bitcast.157), kind=kOutput, calls=%fused_computation.13 | convolution fusion | flops 547356672 | bytes 10485760 | tf_op jit(solution)/shard_map/sgtkwfa,spgtkwfb->spabf/dot_general | solution.py:84
  266.8 8.2 %dynamic_update_slice.12 = bf16[2,2,128,128,128]{2,3,1,4,0:T(8,128)(2,1)} pad(bf16[2,2,128,128,32]{2,3,1,4,0:T(8,128)(2,1)} %fusion, bf16[]{:T(256)} %constant.52.clone.1), padding=0_0x0_0x0_0x0_0x0_96 | pad | bytes 20971522 | tf_op jit(solution)/shard_map/dynamic_update_slice | solution.py:90
  277.9 44.9 %all-gather.9.cloned.1.call-done = bf16[4,64,2,4,32,128]{5,4,3,2,1,0:T(8,128)(2,1)} async-done(((bf16[4,2,2,4,32,128]{5,4,3,2,1,0:T(8,128)(2,1)}), bf16[4,64,2,4,32,128]{5,4,3,2,1,0:T(8,128)(2,1)}) %all-gather.9.cloned.1.call-update) | async-done | bytes 16777232 | tf_op jit(solution)/shard_map/all_gather | solution.py:75
  322.8 6.7 %gather_fusion.4 = bf16[8,4,2,4,32,128]{5,4,3,2,1,0:T(8,128)(2,1)S(1)} fusion(bf16[4,64,2,4,32,128]{5,4,3,2,1,0:T(8,128)(2,1)} %all-gather.9.cloned.1.call-done, s32[1024]{0:T(1024)S(1)} %pad_clamp_fusion.1), kind=kCustom, calls=%fused_computation.4.clone | custom fusion | bytes 4194336 | tf_op jit(solution)/shard_map/jit(_take)/gather | solution.py:79
  329.5 67.5 %all-gather.11.cloned.1.call-done = bf16[4,64,2,4,32,128]{5,4,3,2,1,0:T(8,128)(2,1)} async-done(((bf16[4,2,2,4,32,128]{5,4,3,2,1,0:T(8,128)(2,1)}), bf16[4,64,2,4,32,128]{5,4,3,2,1,0:T(8,128)(2,1)}) %all-gather.11.cloned.1.call-update) | async-done | bytes 16777232 | tf_op jit(solution)/shard_map/all_gather | solution.py:75
  397.1 7.9 %gather_fusion.6 = bf16[8,4,2,4,32,128]{5,4,3,2,1,0:T(8,128)(2,1)} fusion(bf16[4,64,2,4,32,128]{5,4,3,2,1,0:T(8,128)(2,1)} %all-gather.11.cloned.1.call-done, s32[1024]{0:T(1024)S(1)} %pad_clamp_fusion.1), kind=kCustom, calls=%fused_computation.6.clone | custom fusion | bytes 4194336 | tf_op jit(solution)/shard_map/jit(_take)/gather | solution.py:79
  413.1 8.0 %gather_fusion.5 = bf16[8,4,2,4,32,128]{5,4,3,2,1,0:T(8,128)(2,1)} fusion(bf16[4,64,2,4,32,128]{5,4,3,2,1,0:T(8,128)(2,1)} %all-gather.9.cloned.1.call-done, s32[1024]{0:T(1024)S(1)} %pad_clamp_fusion), kind=kCustom, calls=%fused_computation.5.clone | custom fusion | bytes 4194336 | tf_op jit(solution)/shard_map/jit(_take)/gather | solution.py:76
  421.0 7.9 %gather_fusion.7 = bf16[8,4,2,4,32,128]{5,4,3,2,1,0:T(8,128)(2,1)} fusion(bf16[4,64,2,4,32,128]{5,4,3,2,1,0:T(8,128)(2,1)} %all-gather.11.cloned.1.call-done, s32[1024]{0:T(1024)S(1)} %pad_clamp_fusion), kind=kCustom, calls=%fused_computation.7.clone | custom fusion | bytes 4194336 | tf_op jit(solution)/shard_map/jit(_take)/gather | solution.py:76
  428.9 4.9 broadcast_select_fusion
  439.1 9.3 %fusion.3 = bf16[2,2,128,128,128]{2,3,1,4,0:T(8,128)(2,1)} fusion(bf16[2,2,128,128,128]{2,3,1,4,0:T(8,128)(2,1)} %constant_dynamic-update-slice_fusion, bf16[2,1,4,4,2,4,32,128]{7,5,3,4,2,1,6,0:T(4,128)(2,1)} %maximum_bitcast_fusion.3, bf16[2,1,4,4,2,4,32,128]{7,5,3,4,2,1,6,0:T(4,128)(2,1)S(1)} %bitcast.148, ...), kind=kOutput, calls=%fused_computation.15 | convolution fusion | flops 547356672 | bytes 10485760 | tf_op jit(solution)/shard_map/sgtkwfa,spgtkwfb->spabf/dot_general | solution.py:84
  448.4 12.0 %fusion.5 = bf16[2,2,128,128,128]{2,3,1,4,0:T(8,128)(2,1)} fusion(bf16[2,2,128,128,128]{2,3,1,4,0:T(8,128)(2,1)} %fusion.3, bf16[2,1,4,4,2,4,32,128]{7,5,3,4,2,1,6,0:T(4,128)(2,1)S(1)} %copy-done.7, bf16[2,1,4,4,2,4,32,128]{7,5,3,4,2,1,6,0:T(4,128)(2,1)S(1)} %bitcast.146, bf16[2,4,4,2,4,32,128,1]{6,5,4,3,1,2,0,7:T(8,128)(2,1)} %bitcast.158), kind=kOutput, calls=%fused_computation.17 | convolution fusion | flops 547356672 | bytes 10485760 | tf_op jit(solution)/shard_map/sgtkwfa,spgtkwfb->spabf/dot_general | solution.py:84
  460.5 25.8 %copy.56 = bf16[2,2,128,128,128]{4,3,2,1,0:T(8,128)(2,1)} copy(bf16[2,2,128,128,128]{2,3,1,4,0:T(8,128)(2,1)} %fusion.5) | data formatting | bytes 33554432 | tf_op jit(solution)/shard_map/dynamic_update_slice | solution.py:90
  (80 shorter events, 48.3 us)
Async XLA Ops:
  6.5 126.9 %all-gather.5.cloned.1.call-start = ((), (), s32[]{:S(2)}) async-start(), calls=%async_computation.4 | async-start | bytes 17301504 | tf_op jit(solution)/shard_map/all_gather | solution.py:75
  6.5 8.2 %copy-start.13 = (f32[4,256,1024]{2,1,0:T(8,128)S(1)}, f32[4,256,1024]{2,1,0:T(8,128)}, u32[]{:S(2)}) copy-start(f32[4,256,1024]{2,1,0:T(8,128)} %param.5) | copy-start | bytes 12582916
  45.0 28.0 %copy-start.11 = (s32[256]{0:T(256)S(1)}, s32[256]{0:T(256)}, u32[]{:S(2)}) copy-start(s32[256]{0:T(256)} %param.7) | copy-start | bytes 3076
  45.0 29.2 %copy-start.12 = (s32[256,2]{0,1:T(2,128)S(1)}, s32[256,2]{0,1:T(2,128)}, u32[]{:S(2)}) copy-start(s32[256,2]{0,1:T(2,128)} %param.6) | copy-start | bytes 6148
  58.5 149.3 %all-gather.7.cloned.1.call-start = ((), (), s32[]{:S(2)}) async-start(), calls=%async_computation.5 | async-start | bytes 17301504 | tf_op jit(solution)/shard_map/all_gather | solution.py:75
  69.4 180.3 %all-to-all-start = ((bf16[4,2,2,4,32,128]{5,4,3,2,1,0:T(8,128)(2,1)}), bf16[4,2,2,4,32,128]{5,4,3,2,1,0:T(8,128)(2,1)S(1)}, u32[]{:S(2)}, u32[]{:S(2)}) async-start(bf16[4,2,2,4,32,128]{5,4,3,2,1,0:T(8,128)(2,1)} %get-tuple-element.33), calls=%async_computation | async-start | bytes 1048576 | tf_op jit(solution)/shard_map/all_to_all | solution.py:68
  73.0 249.8 %all-gather.9.cloned.1.call-start = ((), (), s32[]{:S(2)}) async-start(), calls=%async_computation.6 | async-start | bytes 17301504 | tf_op jit(solution)/shard_map/all_gather | solution.py:75
  239.5 4.1 copy-start.6
  249.8 0.8 copy-start.8
  250.6 15.4 %all-to-all-start.2 = ((bf16[4,2,2,4,32,128]{5,4,3,2,1,0:T(8,128)(2,1)}), bf16[4,2,2,4,32,128]{5,4,3,2,1,0:T(8,128)(2,1)S(1)}, u32[]{:S(2)}, u32[]{:S(2)}) async-start(bf16[4,2,2,4,32,128]{5,4,3,2,1,0:T(8,128)(2,1)} %get-tuple-element.31), calls=%async_computation.2 | async-start | bytes 1048576 | tf_op jit(solution)/shard_map/all_to_all | solution.py:68
  254.6 142.5 %all-gather.11.cloned.1.call-start = ((), (), s32[]{:S(2)}) async-start(), calls=%async_computation.7 | async-start | bytes 17301504 | tf_op jit(solution)/shard_map/all_gather | solution.py:75
  258.0 1.7 copy-start.10
  266.0 0.8 copy-start.9
  266.8 8.2 %copy-start.2 = (bf16[2,2,128,128,32]{2,3,1,4,0:T(8,128)(2,1)S(1)}, bf16[2,2,128,128,32]{2,3,1,4,0:T(8,128)(2,1)}, u32[]{:S(2)}) copy-start(bf16[2,2,128,128,32]{2,3,1,4,0:T(8,128)(2,1)} %fusion.1) | copy-start | bytes 12582916
  409.2 2.1 copy-start
  428.9 4.9 copy-start.4
  428.9 4.9 copy-start.5
  433.8 2.7 copy-start.3
  436.5 2.7 copy-start.1
  439.1 9.3 %copy-start.7 = (bf16[2,1,4,4,2,4,32,128]{7,5,3,4,2,1,6,0:T(4,128)(2,1)S(1)}, bf16[2,1,4,4,2,4,32,128]{7,5,3,4,2,1,6,0:T(4,128)(2,1)}, u32[]{:S(2)}) copy-start(bf16[2,1,4,4,2,4,32,128]{7,5,3,4,2,1,6,0:T(4,128)(2,1)} %maximum_bitcast_fusion.4) | copy-start | bytes 6291460
Sparse Core Ops, SparseCore 0:
  58.7 74.7 all-gather.4
  135.7 72.0 all-gather.6
  250.7 72.0 all-gather.8
  325.0 72.0 all-gather.10
